TPU v7x, 256 devices: a whole 4x4x8 slice. The times are simulated.
256 devices in a mesh: probe: 16 (over z, x_lo), slab: 16 (over x_hi, y, core).
Axes of the slice: x: 4 (x_hi: 2, x_lo: 2; x = x_hi * 2 + x_lo), y: 4, z: 8, core: 2. Of those that a mesh axis runs over, the one named last changes fastest.
Arguments:
- u_prev: float32 [512, 128, 128], P('slab', 'probe'), may hold values from -6 to 6
- u_cur: float32 [512, 128, 128], P('slab', 'probe'), may hold values from -6 to 6
- buoyancy: float32 [512, 128, 128], P('slab'), may hold values from 0.6 to 1.4
- kappa: float32 [512, 128, 128], P('slab'), may hold values from 0.06 to 0.14
- dkappa: float32 [16, 512, 128, 128], P('probe', 'slab'), may hold values from -0.3 to 0.3
- du_prev: float32 [16, 512, 128, 128], P('probe', 'slab'), may hold values from -6 to 6
- du_cur: float32 [16, 512, 128, 128], P('probe', 'slab'), may hold values from -6 to 6
Outputs:
- background_first: float32 [512, 128, 128], P('slab', 'probe')
- background_second: float32 [512, 128, 128], P('slab', 'probe')
- born_first: float32 [16, 512, 128, 128], P('probe', 'slab')
- born_second: float32 [16, 512, 128, 128], P('probe', 'slab')
All inputs are finite; a program needn't handle non-finite values.
Results may differ from a plain program's by a relative error of at most 0.00002.
Values sent between devices are 32-bit elements; how exact they have to be, the bound alone decides.
No kernel may reach another device: no remote copies, remote signals or barrier semaphores. Data moves between devices by JAX's collectives and lax.ppermute only.
A program may use at most 128 MiB of HBM per device.

v0:
```python
import jax
import jax.numpy as jnp
from jax import lax
from jax.sharding import PartitionSpec as P

SECOND = (-205.0 / 72.0, 8.0 / 5.0, -1.0 / 5.0, 8.0 / 315.0, -1.0 / 560.0)
FIRST = (0.0, 4.0 / 5.0, -1.0 / 5.0, 4.0 / 105.0, -1.0 / 280.0)


def extended_2(cells, sides, width):
    for axis, dim in sides:
        count = lax.axis_size(axis)
        ends = count - 1
        head = lax.slice_in_dim(cells, 0, width, axis=dim)
        tail = lax.slice_in_dim(cells, cells.shape[dim] - width, cells.shape[dim], axis=dim)
        cells = jnp.concatenate(
            [
                lax.ppermute(tail, axis, [(i, (i + 1) % count) for i in range(ends)]),
                cells,
                lax.ppermute(head, axis, [((i + 1) % count, i) for i in range(ends)]),
            ],
            axis=dim,
        )
    return cells


def derivatives(extended):
    array_rank = extended.ndim
    center = extended[..., 4:-4, 4:-4, 4:-4]
    cores = (
        extended[..., :, 4:-4, 4:-4],
        extended[..., 4:-4, :, 4:-4],
        extended[..., 4:-4, 4:-4, :],
    )
    second = 3.0 * SECOND[0] * center
    gradients = []
    for dimension in range(3):
        source = cores[dimension]
        axis_place = array_rank - 3 + dimension
        extent = center.shape[axis_place]
        gradient = jnp.zeros_like(center)
        for distance in range(1, 5):
            higher = lax.slice_in_dim(source, 4 + distance, 4 + distance + extent, axis=axis_place)
            deeper = lax.slice_in_dim(source, 4 - distance, 4 - distance + extent, axis=axis_place)
            second = second + SECOND[distance] * (higher + deeper)
            gradient = gradient + FIRST[distance] * (higher - deeper)
        gradients.append(gradient)
    return (second, gradients[0], gradients[1], gradients[2])


def operate(extended, buoyancy, slopes):
    second, depth_slope, cross_slope, lateral_slope = derivatives(extended)
    return (
        buoyancy * second
        + slopes[0] * depth_slope
        + slopes[1] * cross_slope
        + slopes[2] * lateral_slope
    )


def local(u_prev, u_cur, buoyancy, kappa, dkappa, du_prev, du_cur):
    strip = u_cur.shape[1]
    offset = lax.axis_index("probe") * strip
    rimmed = extended_2(buoyancy, (("slab", 0),), 4)
    buoyancy_widths = [(0, 0), (4, 4), (4, 4)]
    unused, slope_one, slope_two, slope_three = derivatives(jnp.pad(rimmed, buoyancy_widths))
    slopes = (slope_one, slope_two, slope_three)
    probe_kappa = dkappa[0]
    older = du_prev[0]
    newer = du_cur[0]
    born_states = []
    background_states = []

    def cut_strip(field):
        return lax.dynamic_slice_in_dim(field, offset, strip, 1)

    strip_buoyancy = cut_strip(buoyancy)
    strip_kappa = cut_strip(kappa)
    strip_slopes = (cut_strip(slope_one), cut_strip(slope_two), cut_strip(slope_three))
    background_old = u_prev
    background_new = u_cur
    for repeat in range(2):
        extended = extended_2(background_new, (("probe", 1), ("slab", 0)), 4)
        extended = jnp.pad(extended, [(0, 0), (0, 0), (4, 4)])
        image_strip = operate(extended, strip_buoyancy, strip_slopes)
        background_next = 2.0 * background_new - background_old + strip_kappa * image_strip
        image_whole = lax.all_gather(image_strip, "probe", axis=1, tiled=True)
        born_rimmed = extended_2(newer, (("slab", 0),), 4)
        born_image = operate(jnp.pad(born_rimmed, [(0, 0), (4, 4), (4, 4)]), buoyancy, slopes)
        born_next = 2.0 * newer - older + kappa * born_image + probe_kappa * image_whole
        background_states.append(background_next)
        born_states.append(born_next)
        background_old, background_new = (background_new, background_next)
        older, newer = (newer, born_next)
    return (background_states[0], background_states[1], born_states[0][None], born_states[1][None])


def solution(mesh):
    return jax.shard_map(
        local,
        mesh=mesh,
        in_specs=(
            P("slab", "probe", None),
            P("slab", "probe", None),
            P("slab", None, None),
            P("slab", None, None),
            P("probe", "slab", None, None),
            P("probe", "slab", None, None),
            P("probe", "slab", None, None),
        ),
        out_specs=(
            P("slab", "probe", None),
            P("slab", "probe", None),
            P("probe", "slab", None, None),
            P("probe", "slab", None, None),
        ),
        check_vma=False,
    )
```

profile of v0, /device:TPU:6, one launch (start us, length us, event | category | flops | bytes accessed | tf_op | source)
XLA Modules:
  0.0 289.8 jit_solution(7251088802055237671)
XLA Ops:
  8.3 5.2 %collective-permute-start.4 = (f32[4,128,128]{2,1,0:T(8,128)S(1)}, f32[4,128,128]{2,1,0:T(8,128)S(1)}, u32[]{:S(2)}, u32[]{:S(2)}) collective-permute-start(f32[4,128,128]{2,1,0:T(8,128)S(1)} %get-tuple-element.17), channel_id=1, source_target_pairs={{1,0},{2,1},{3,2},{4,3},{5,4},{6,5},{7,6},{8,7},{9,8},{10,9},{11,1... | collective-permute-start | bytes 786440 | tf_op jit(solution)/shard_map/ppermute | solution.py:20
  13.5 1.9 collective-permute-start.5
  16.5 1.9 collective-permute-start.1
  18.4 4.8 %collective-permute-start = (f32[32,4,128]{2,1,0:T(4,128)S(1)}, f32[32,4,128]{2,1,0:T(4,128)S(1)}, u32[]{:S(2)}, u32[]{:S(2)}) collective-permute-start(f32[32,4,128]{2,1,0:T(4,128)S(1)} %get-tuple-element.28), channel_id=1, source_target_pairs={{0,16},{16,32},{32,48},{48,64},{64,80},{80,96},{96,112},{112,128},... | collective-permute-start | bytes 196616 | tf_op jit(solution)/shard_map/ppermute | solution.py:18
  25.9 6.1 %collective-permute-start.2 = (f32[4,16,128]{2,1,0:T(8,128)S(1)}, f32[4,16,128]{2,1,0:T(8,128)S(1)}, u32[]{:S(2)}, u32[]{:S(2)}) collective-permute-start(f32[4,16,128]{2,1,0:T(8,128)S(1)} %get-tuple-element.25), channel_id=1, source_target_pairs={{1,0},{2,1},{3,2},{4,3},{5,4},{6,5},{7,6},{8,7},{9,8},{10,9},{11,1... | collective-permute-start | bytes 98312 | tf_op jit(solution)/shard_map/ppermute | solution.py:20
  32.0 1.9 collective-permute-start.3
  34.7 6.2 %collective-permute-done.3 = f32[4,16,128]{2,1,0:T(8,128)S(1)} collective-permute-done((f32[4,16,128]{2,1,0:T(8,128)S(1)}, f32[4,16,128]{2,1,0:T(8,128)S(1)}, u32[]{:S(2)}, u32[]{:S(2)}) %collective-permute-start.3) | collective-permute-done | bytes 32800 | tf_op jit(solution)/shard_map/ppermute | solution.py:18
  42.7 4.6 %select_maximum_fusion.4 = f32[40,136,136]{2,1,0:T(8,128)S(1)} fusion(f32[4,128,128]{2,1,0:T(8,128)} %copy-done.8, f32[32,128,128]{2,1,0:T(8,128)S(1)} %copy-done, f32[4,128,128]{2,1,0:T(8,128)} %collective-permute-done.5), kind=kLoop, calls=%fused_computation.8 | loop fusion | flops 11097600 | bytes 5580800 | tf_op jit(solution)/shard_map/concatenate | solution.py:16
  47.3 9.8 %fusion.23 = (f32[32,128,128]{2,1,0:T(8,128)}, f32[32,128,128]{2,1,0:T(8,128)}) fusion(f32[40,136,136]{2,1,0:T(8,128)S(1)} %select_maximum_fusion.4), kind=kLoop, calls=%fused_computation.66 | loop fusion | flops 11534336 | bytes 37748736 | tf_op jit(solution)/shard_map/add | solution.py:46
  58.1 2.1 constant_dynamic-update-slice_fusion.3
  60.3 2.0 fusion.30
  62.3 1.4 copy-done.2
  63.7 2.3 multiply_add_fusion.2
  67.1 1.9 collective-permute-start.10
  69.0 2.4 collective-permute-start.11
  71.5 1.9 collective-permute-start.7
  73.4 4.8 %collective-permute-start.6 = (f32[32,4,128]{2,1,0:T(4,128)S(1)}, f32[32,4,128]{2,1,0:T(4,128)S(1)}, u32[]{:S(2)}, u32[]{:S(2)}) collective-permute-start(f32[32,4,128]{2,1,0:T(4,128)S(1)} %get-tuple-element.26), channel_id=1, source_target_pairs={{0,16},{16,32},{32,48},{48,64},{64,80},{80,96},{96,112},{112,128},... | collective-permute-start | bytes 196616 | tf_op jit(solution)/shard_map/ppermute | solution.py:18
  78.6 2.4 collective-permute-done.6
  81.0 5.2 %collective-permute-start.8 = (f32[4,16,128]{2,1,0:T(8,128)S(1)}, f32[4,16,128]{2,1,0:T(8,128)S(1)}, u32[]{:S(2)}, u32[]{:S(2)}) collective-permute-start(f32[4,16,128]{2,1,0:T(8,128)S(1)} %get-tuple-element.21), channel_id=1, source_target_pairs={{1,0},{2,1},{3,2},{4,3},{5,4},{6,5},{7,6},{8,7},{9,8},{10,9},{11,1... | collective-permute-start | bytes 98312 | tf_op jit(solution)/shard_map/ppermute | solution.py:20
  86.3 2.1 collective-permute-start.9
  88.4 6.5 %select_maximum_fusion.2 = f32[40,136,136]{2,1,0:T(8,128)} fusion(f32[4,128,128]{2,1,0:T(8,128)S(1)} %collective-permute-done.10, f32[32,128,128]{2,1,0:T(8,128)} %bitcast.24, f32[4,128,128]{2,1,0:T(8,128)S(1)} %collective-permute-done.11), kind=kLoop, calls=%fused_computation.6 | loop fusion | flops 11097600 | bytes 5580800 | tf_op jit(solution)/shard_map/concatenate | solution.py:16
  94.9 1.2 collective-permute-done.9
  96.6 2.4 multiply_add_fusion
  99.0 53.2 %all-gather.3.cloned.1.call-done = f32[32,128,128]{2,1,0:T(8,128)} async-done(((f32[32,8,128]{2,1,0:T(8,128)}), f32[32,128,128]{2,1,0:T(8,128)}) %all-gather.3.cloned.1.call-update) | async-done | bytes 2097168 | tf_op jit(solution)/shard_map/all_gather | solution.py:87
  152.3 48.3 %fusion.36 = f32[32,128,128]{2,1,0:T(8,128)} fusion(f32[32,128,128]{2,1,0:T(8,128)} %all-gather.3.cloned.1.call-done, f32[1,32,128,128]{3,2,1,0:T(8,128)} %param.11, f32[1,32,128,128]{3,2,1,0:T(8,128)} %param.12, f32[32,128,128]{2,1,0:T(8,128)} %param.10, f32[32,128,128]{2,1,0:T(8,128)} %get-tuple-element.9, f32[32,128,128]{2,1,0:T(8,128)} %get-tuple-element.8, ...), kind=kLoop, calls=%fused_computation.88 | loop fusion | flops 47710208 | bytes 55050240 | tf_op jit(solution)/shard_map/add | solution.py:90
  201.6 1.9 collective-permute-start.12
  203.6 2.6 collective-permute-start.13
  206.2 6.6 %collective-permute-done.12 = f32[4,128,128]{2,1,0:T(8,128)S(1)} collective-permute-done((f32[4,128,128]{2,1,0:T(8,128)S(1)}, f32[4,128,128]{2,1,0:T(8,128)S(1)}, u32[]{:S(2)}, u32[]{:S(2)}) %collective-permute-start.12) | collective-permute-done | bytes 262176 | tf_op jit(solution)/shard_map/ppermute | solution.py:20
  212.8 5.7 %collective-permute-done.13 = f32[4,128,128]{2,1,0:T(8,128)S(1)} collective-permute-done((f32[4,128,128]{2,1,0:T(8,128)S(1)}, f32[4,128,128]{2,1,0:T(8,128)S(1)}, u32[]{:S(2)}, u32[]{:S(2)}) %collective-permute-start.13) | collective-permute-done | bytes 262176 | tf_op jit(solution)/shard_map/ppermute | solution.py:18
  218.5 6.5 %select_maximum_fusion = f32[40,136,136]{2,1,0:T(8,128)} fusion(f32[4,128,128]{2,1,0:T(8,128)S(1)} %collective-permute-done.12, f32[32,128,128]{2,1,0:T(8,128)} %fusion.36, f32[4,128,128]{2,1,0:T(8,128)S(1)} %collective-permute-done.13), kind=kLoop, calls=%fused_computation.4 | loop fusion | flops 11097600 | bytes 5580800 | tf_op jit(solution)/shard_map/concatenate | solution.py:16
  225.0 8.6 %all-gather.5.cloned.1.call-done = f32[32,128,128]{2,1,0:T(8,128)} async-done(((f32[32,8,128]{2,1,0:T(8,128)}), f32[32,128,128]{2,1,0:T(8,128)}) %all-gather.5.cloned.1.call-update) | async-done | bytes 2097168 | tf_op jit(solution)/shard_map/all_gather | solution.py:87
  233.6 49.3 %fusion.38 = f32[1,32,128,128]{3,2,1,0:T(8,128)} fusion(f32[32,128,128]{2,1,0:T(8,128)} %all-gather.5.cloned.1.call-done, f32[1,32,128,128]{3,2,1,0:T(8,128)} %param.11, f32[32,128,128]{2,1,0:T(8,128)} %param.10, f32[32,128,128]{2,1,0:T(8,128)} %get-tuple-element.9, f32[32,128,128]{2,1,0:T(8,128)} %get-tuple-element.8, f32[32,128,128]{2,1,0:T(8,128)} %copy-done.2, ...), kind=kLoop, calls=%fused_computation.90 | loop fusion | flops 47710208 | bytes 55050240 | tf_op jit(solution)/shard_map/broadcast_in_dim | solution.py:95
  (49 shorter events, 11.4 us)
Async XLA Ops:
  7.2 33.7 %copy-start.3 = (f32[32,8,128]{2,1,0:T(8,128)S(1)}, f32[32,8,128]{2,1,0:T(8,128)}, u32[]{:S(2)}) copy-start(f32[32,8,128]{2,1,0:T(8,128)} %param.8) | copy-start | bytes 393220
  7.2 145.1 %all-gather.3.cloned.1.call-start = ((), (), s32[]{:S(2)}) async-start(), calls=%async_computation | async-start | bytes 2228224 | tf_op jit(solution)/shard_map/all_gather | solution.py:87
  8.3 33.7 %collective-permute-start.4 = (f32[4,128,128]{2,1,0:T(8,128)S(1)}, f32[4,128,128]{2,1,0:T(8,128)S(1)}, u32[]{:S(2)}, u32[]{:S(2)}) collective-permute-start(f32[4,128,128]{2,1,0:T(8,128)S(1)} %get-tuple-element.17), channel_id=1, source_target_pairs={{1,0},{2,1},{3,2},{4,3},{5,4},{6,5},{7,6},{8,7},{9,8},{10,9},{11,1... | collective-permute-start | bytes 786440 | tf_op jit(solution)/shard_map/ppermute | solution.py:20
  13.5 29.2 %collective-permute-start.5 = (f32[4,128,128]{2,1,0:T(8,128)S(1)}, f32[4,128,128]{2,1,0:T(8,128)}, u32[]{:S(2)}, u32[]{:S(2)}) collective-permute-start(f32[4,128,128]{2,1,0:T(8,128)S(1)} %get-tuple-element.16), channel_id=1, source_target_pairs={{0,1},{1,2},{2,3},{3,4},{4,5},{5,6},{6,7},{7,8},{8,9},{9,10},{10,1... | collective-permute-start | bytes 786440 | tf_op jit(solution)/shard_map/ppermute | solution.py:18
  16.5 7.8 %collective-permute-start.1 = (f32[32,4,128]{2,1,0:T(4,128)S(1)}, f32[32,4,128]{2,1,0:T(4,128)S(1)}, u32[]{:S(2)}, u32[]{:S(2)}) collective-permute-start(f32[32,4,128]{2,1,0:T(4,128)S(1)} %get-tuple-element.29), channel_id=1, source_target_pairs={{16,0},{32,16},{48,32},{64,48},{80,64},{96,80},{112,96},{128,112},... | collective-permute-start | bytes 196616 | tf_op jit(solution)/shard_map/ppermute | solution.py:20
  18.4 6.7 %collective-permute-start = (f32[32,4,128]{2,1,0:T(4,128)S(1)}, f32[32,4,128]{2,1,0:T(4,128)S(1)}, u32[]{:S(2)}, u32[]{:S(2)}) collective-permute-start(f32[32,4,128]{2,1,0:T(4,128)S(1)} %get-tuple-element.28), channel_id=1, source_target_pairs={{0,16},{16,32},{32,48},{48,64},{64,80},{80,96},{96,112},{112,128},... | collective-permute-start | bytes 196616 | tf_op jit(solution)/shard_map/ppermute | solution.py:18
  23.2 19.5 %copy-start = (f32[32,128,128]{2,1,0:T(8,128)S(1)}, f32[32,128,128]{2,1,0:T(8,128)}, u32[]{:S(2)}) copy-start(f32[32,128,128]{2,1,0:T(8,128)} %param.9) | copy-start | bytes 6291460
  25.9 8.1 %collective-permute-start.2 = (f32[4,16,128]{2,1,0:T(8,128)S(1)}, f32[4,16,128]{2,1,0:T(8,128)S(1)}, u32[]{:S(2)}, u32[]{:S(2)}) collective-permute-start(f32[4,16,128]{2,1,0:T(8,128)S(1)} %get-tuple-element.25), channel_id=1, source_target_pairs={{1,0},{2,1},{3,2},{4,3},{5,4},{6,5},{7,6},{8,7},{9,8},{10,9},{11,1... | collective-permute-start | bytes 98312 | tf_op jit(solution)/shard_map/ppermute | solution.py:20
  32.0 8.8 %collective-permute-start.3 = (f32[4,16,128]{2,1,0:T(8,128)S(1)}, f32[4,16,128]{2,1,0:T(8,128)S(1)}, u32[]{:S(2)}, u32[]{:S(2)}) collective-permute-start(f32[4,16,128]{2,1,0:T(8,128)S(1)} %get-tuple-element.24), channel_id=1, source_target_pairs={{0,1},{1,2},{2,3},{3,4},{4,5},{5,6},{6,7},{7,8},{8,9},{9,10},{10,1... | collective-permute-start | bytes 98312 | tf_op jit(solution)/shard_map/ppermute | solution.py:18
  34.0 0.7 copy-start.6
  42.0 0.7 copy-start.8
  58.1 2.2 copy-start.9
  60.3 3.4 %copy-start.1 = (f32[32,128,128]{2,1,0:T(8,128)S(1)}, f32[32,128,128]{2,1,0:T(8,128)}, u32[]{:S(2)}) copy-start(f32[32,128,128]{2,1,0:T(8,128)} %param.9) | copy-start | bytes 6291460
  60.3 3.4 %copy-start.5 = (f32[36,16,128]{2,1,0:T(8,128)S(1)}, f32[36,16,128]{2,1,0:T(8,128)}, u32[]{:S(2)}) copy-start(f32[36,16,128]{2,1,0:T(8,128)} %get-tuple-element.23) | copy-start | bytes 884740
  60.3 3.4 %copy-start.7 = (f32[32,12,128]{2,1,0:T(8,128)S(1)}, f32[32,12,128]{2,1,0:T(8,128)}, u32[]{:S(2)}) copy-start(f32[32,12,128]{2,1,0:T(8,128)} %copy-done.6) | copy-start | bytes 589828
  60.3 3.4 %copy-start.10 = (f32[32,8,128]{2,1,0:T(8,128)S(1)}, f32[32,8,128]{2,1,0:T(8,128)}, u32[]{:S(2)}) copy-start(f32[32,8,128]{2,1,0:T(8,128)} %param.7) | copy-start | bytes 393220
  62.3 1.4 copy-start.2
  66.0 30.6 %copy-start.4 = (f32[32,8,128]{2,1,0:T(8,128)}, f32[32,8,128]{2,1,0:T(8,128)S(1)}, u32[]{:S(2)}) copy-start(f32[32,8,128]{2,1,0:T(8,128)S(1)} %get-tuple-element.6) | copy-start | bytes 393220
  66.0 167.6 %all-gather.5.cloned.1.call-start = ((), (), s32[]{:S(2)}) async-start(), calls=%async_computation.1 | async-start | bytes 2228224 | tf_op jit(solution)/shard_map/all_gather | solution.py:87
  67.1 21.3 %collective-permute-start.10 = (f32[4,128,128]{2,1,0:T(8,128)S(1)}, f32[4,128,128]{2,1,0:T(8,128)S(1)}, u32[]{:S(2)}, u32[]{:S(2)}) collective-permute-start(f32[4,128,128]{2,1,0:T(8,128)S(1)} %get-tuple-element.13), channel_id=1, source_target_pairs={{1,0},{2,1},{3,2},{4,3},{5,4},{6,5},{7,6},{8,7},{9,8},{10,9},{11,1... | collective-permute-start | bytes 786440 | tf_op jit(solution)/shard_map/ppermute | solution.py:20
  69.0 19.4 %collective-permute-start.11 = (f32[4,128,128]{2,1,0:T(8,128)S(1)}, f32[4,128,128]{2,1,0:T(8,128)S(1)}, u32[]{:S(2)}, u32[]{:S(2)}) collective-permute-start(f32[4,128,128]{2,1,0:T(8,128)S(1)} %get-tuple-element.12), channel_id=1, source_target_pairs={{0,1},{1,2},{2,3},{3,4},{4,5},{5,6},{6,7},{7,8},{8,9},{9,10},{10,1... | collective-permute-start | bytes 786440 | tf_op jit(solution)/shard_map/ppermute | solution.py:18
  71.5 7.1 %collective-permute-start.7 = (f32[32,4,128]{2,1,0:T(4,128)S(1)}, f32[32,4,128]{2,1,0:T(4,128)S(1)}, u32[]{:S(2)}, u32[]{:S(2)}) collective-permute-start(f32[32,4,128]{2,1,0:T(4,128)S(1)} %get-tuple-element.27), channel_id=1, source_target_pairs={{16,0},{32,16},{48,32},{64,48},{80,64},{96,80},{112,96},{128,112},... | collective-permute-start | bytes 196616 | tf_op jit(solution)/shard_map/ppermute | solution.py:20
  73.4 7.6 %collective-permute-start.6 = (f32[32,4,128]{2,1,0:T(4,128)S(1)}, f32[32,4,128]{2,1,0:T(4,128)S(1)}, u32[]{:S(2)}, u32[]{:S(2)}) collective-permute-start(f32[32,4,128]{2,1,0:T(4,128)S(1)} %get-tuple-element.26), channel_id=1, source_target_pairs={{0,16},{16,32},{32,48},{48,64},{64,80},{80,96},{96,112},{112,128},... | collective-permute-start | bytes 196616 | tf_op jit(solution)/shard_map/ppermute | solution.py:18
  81.0 13.9 %collective-permute-start.8 = (f32[4,16,128]{2,1,0:T(8,128)S(1)}, f32[4,16,128]{2,1,0:T(8,128)S(1)}, u32[]{:S(2)}, u32[]{:S(2)}) collective-permute-start(f32[4,16,128]{2,1,0:T(8,128)S(1)} %get-tuple-element.21), channel_id=1, source_target_pairs={{1,0},{2,1},{3,2},{4,3},{5,4},{6,5},{7,6},{8,7},{9,8},{10,9},{11,1... | collective-permute-start | bytes 98312 | tf_op jit(solution)/shard_map/ppermute | solution.py:20
  86.3 9.8 %collective-permute-start.9 = (f32[4,16,128]{2,1,0:T(8,128)S(1)}, f32[4,16,128]{2,1,0:T(8,128)S(1)}, u32[]{:S(2)}, u32[]{:S(2)}) collective-permute-start(f32[4,16,128]{2,1,0:T(8,128)S(1)} %get-tuple-element.20), channel_id=1, source_target_pairs={{0,1},{1,2},{2,3},{3,4},{4,5},{5,6},{6,7},{7,8},{8,9},{9,10},{10,1... | collective-permute-start | bytes 98312 | tf_op jit(solution)/shard_map/ppermute | solution.py:18
  201.6 11.1 %collective-permute-start.12 = (f32[4,128,128]{2,1,0:T(8,128)S(1)}, f32[4,128,128]{2,1,0:T(8,128)S(1)}, u32[]{:S(2)}, u32[]{:S(2)}) collective-permute-start(f32[4,128,128]{2,1,0:T(8,128)S(1)} %get-tuple-element.11), channel_id=1, source_target_pairs={{1,0},{2,1},{3,2},{4,3},{5,4},{6,5},{7,6},{8,7},{9,8},{10,9},{11,1... | collective-permute-start | bytes 786440 | tf_op jit(solution)/shard_map/ppermute | solution.py:20
  203.6 14.9 %collective-permute-start.13 = (f32[4,128,128]{2,1,0:T(8,128)S(1)}, f32[4,128,128]{2,1,0:T(8,128)S(1)}, u32[]{:S(2)}, u32[]{:S(2)}) collective-permute-start(f32[4,128,128]{2,1,0:T(8,128)S(1)} %get-tuple-element.10), channel_id=1, source_target_pairs={{0,1},{1,2},{2,3},{3,4},{4,5},{5,6},{6,7},{7,8},{8,9},{9,10},{10,1... | collective-permute-start | bytes 786440 | tf_op jit(solution)/shard_map/ppermute | solution.py:18
Sparse Core Ops, SparseCore 0:
  66.1 86.1 all-gather.2
  154.0 79.5 all-gather.4
where the time goes:
time: 291 us; the launch traced here: 290 us
  other arithmetic  134 us (46%)
  waiting for transfers between devices  85.2 us (29%)
  starting transfers between devices  45 us (15%)
  between operations  14.4 us (5%)
  local copies, waits for them, and re-layouts  11.3 us (4%)
    all_gather x2, waiting for transfers between devices, local(): image_whole = lax.all_gather(image_strip, 'probe', axis=1, tiled=True)  61.9 us
    broadcast_in_dim x1, other arithmetic, local(): born_states[1][None]  49.3 us
    add x1, other arithmetic, local(): 2.0 * newer - older + kappa * born_image + probe_kappa * image_whole  48.3 us
    ppermute x7, starting transfers between devices, extended_2(): lax.ppermute(head, axis, [((i + 1) % count, i) for i in range(ends)])  24.3 us
    ppermute x7, starting transfers between devices, extended_2(): lax.ppermute(tail, axis, [(i, (i + 1) % count) for i in range(ends)])  20.6 us
    concatenate x9, other arithmetic, extended_2(): jnp.concatenate([lax.ppermute(tail, axis, [(i, (i + 1) % count) for i in...  19.9 us
    ppermute x7, waiting for transfers between devices, extended_2(): lax.ppermute(tail, axis, [(i, (i + 1) % count) for i in range(ends)])  16.3 us
    add x2, other arithmetic, derivatives(): gradient = gradient + FIRST[distance] * (higher - deeper)  11.8 us
  transfers between devices with their start and end apart: 16, of which 9 were waited for; matrix products, arithmetic and copies ran while one was open for 24% of the time, Pallas kernels for 0%

commit v1 on v0

--- a/solution.py
+++ b/solution.py
@@ -84,7 +84,14 @@
         extended = jnp.pad(extended, [(0, 0), (0, 0), (4, 4)])
         image_strip = operate(extended, strip_buoyancy, strip_slopes)
         background_next = 2.0 * background_new - background_old + strip_kappa * image_strip
-        image_whole = lax.all_gather(image_strip, "probe", axis=1, tiled=True)
+
+        def patch_settle(inp):
+            heard = tuple((inp for _ in range(jax.lax.axis_size("probe"))))
+            s_next = jax.lax.all_to_all(jnp.stack(heard, 0), "probe", 0, 0)
+            arr_now = jnp.concatenate(s_next, 1)
+            return arr_now
+
+        image_whole = patch_settle(image_strip)
         born_rimmed = extended_2(newer, (("slab", 0),), 4)
         born_image = operate(jnp.pad(born_rimmed, [(0, 0), (4, 4), (4, 4)]), buoyancy, slopes)
         born_next = 2.0 * newer - older + kappa * born_image + probe_kappa * image_whole

time: 291 us -> 261 us (0.90)
  waiting for transfers between devices: 85.2 us -> 48 us
  starting transfers between devices: 45 us -> 63.7 us
  between operations: 14.4 us -> 1.18 us
  local copies, waits for them, and re-layouts: 11.3 us -> 14.4 us
    all_gather x2 -> x0, waiting for transfers between devices: 61.9 us -> none  [local(): image_whole = lax.all_gather(image_strip, 'probe', axis=1, tiled=True)]
    ppermute x7, waiting for transfers between devices: 6.94 us -> 33.4 us  [extended_2(): lax.ppermute(head, axis, [((i + 1) % count, i) for i in range(ends)])]
    all_to_all x0 -> x2, starting transfers between devices: none -> 16.3 us  [patch_settle(): s_next = jax.lax.all_to_all(jnp.stack(heard, 0), 'probe', 0, 0)]
    ppermute x7, starting transfers between devices: 24.3 us -> 27.5 us  [extended_2(): lax.ppermute(head, axis, [((i + 1) % count, i) for i in range(ends)])]
    another operation x0 -> x2, local copies, waits for them, and re-layouts: none -> 3.08 us  [patch_settle(): s_next = jax.lax.all_to_all(jnp.stack(heard, 0), 'probe', 0, 0)]
  transfers between devices with their start and end apart: 16 -> 16, of which waited for: 9 -> 6; matrix products, arithmetic and copies ran while one was open for 24% -> 27% of each run, Pallas kernels for 0% -> 0%
where the time goes in v1:
time: 261 us; the launch traced here: 260 us
  other arithmetic  132 us (51%)
  starting transfers between devices  63.7 us (24%)
  waiting for transfers between devices  48 us (18%)
  local copies, waits for them, and re-layouts  14.4 us (6%)
    broadcast_in_dim x1, other arithmetic, local(): born_states[1][None]  48.8 us
    add x1, other arithmetic, local(): 2.0 * newer - older + kappa * born_image + probe_kappa * image_whole  47.9 us
    ppermute x7, waiting for transfers between devices, extended_2(): lax.ppermute(head, axis, [((i + 1) % count, i) for i in range(ends)])  33.4 us
    ppermute x7, starting transfers between devices, extended_2(): lax.ppermute(head, axis, [((i + 1) % count, i) for i in range(ends)])  27.5 us
    ppermute x7, starting transfers between devices, extended_2(): lax.ppermute(tail, axis, [(i, (i + 1) % count) for i in range(ends)])  20 us
    concatenate x9, other arithmetic, extended_2(): jnp.concatenate([lax.ppermute(tail, axis, [(i, (i + 1) % count) for i in...  19.9 us
    all_to_all x2, starting transfers between devices, patch_settle(): s_next = jax.lax.all_to_all(jnp.stack(heard, 0), 'probe', 0, 0)  16.3 us
    ppermute x7, waiting for transfers between devices, extended_2(): lax.ppermute(tail, axis, [(i, (i + 1) % count) for i in range(ends)])  14.6 us
  transfers between devices with their start and end apart: 16, of which 6 were waited for; matrix products, arithmetic and copies ran while one was open for 27% of the time, Pallas kernels for 0%

profile of v1, /device:TPU:6, one launch (start us, length us, event | category | flops | bytes accessed | tf_op | source)
XLA Modules:
  0.0 259.6 jit_solution(11907586964205626632)
XLA Ops:
  1.8 5.2 %collective-permute-start.4 = (f32[4,128,128]{2,1,0:T(8,128)S(1)}, f32[4,128,128]{2,1,0:T(8,128)S(1)}, u32[]{:S(2)}, u32[]{:S(2)}) collective-permute-start(f32[4,128,128]{2,1,0:T(8,128)S(1)} %get-tuple-element.17), channel_id=1, source_target_pairs={{1,0},{2,1},{3,2},{4,3},{5,4},{6,5},{7,6},{8,7},{9,8},{10,9},{11,1... | collective-permute-start | bytes 786440 | tf_op jit(solution)/shard_map/ppermute | solution.py:20
  7.0 1.9 collective-permute-start.5
  9.9 1.9 collective-permute-start.1
  11.8 4.8 %collective-permute-start = (f32[32,4,128]{2,1,0:T(4,128)S(1)}, f32[32,4,128]{2,1,0:T(4,128)S(1)}, u32[]{:S(2)}, u32[]{:S(2)}) collective-permute-start(f32[32,4,128]{2,1,0:T(4,128)S(1)} %get-tuple-element.28), channel_id=1, source_target_pairs={{0,16},{16,32},{32,48},{48,64},{64,80},{80,96},{96,112},{112,128},... | collective-permute-start | bytes 196616 | tf_op jit(solution)/shard_map/ppermute | solution.py:18
  19.3 6.1 %collective-permute-start.2 = (f32[4,16,128]{2,1,0:T(8,128)S(1)}, f32[4,16,128]{2,1,0:T(8,128)S(1)}, u32[]{:S(2)}, u32[]{:S(2)}) collective-permute-start(f32[4,16,128]{2,1,0:T(8,128)S(1)} %get-tuple-element.25), channel_id=1, source_target_pairs={{1,0},{2,1},{3,2},{4,3},{5,4},{6,5},{7,6},{8,7},{9,8},{10,9},{11,1... | collective-permute-start | bytes 98312 | tf_op jit(solution)/shard_map/ppermute | solution.py:20
  25.4 1.9 collective-permute-start.3
  28.1 6.2 %collective-permute-done.3 = f32[4,16,128]{2,1,0:T(8,128)S(1)} collective-permute-done((f32[4,16,128]{2,1,0:T(8,128)S(1)}, f32[4,16,128]{2,1,0:T(8,128)S(1)}, u32[]{:S(2)}, u32[]{:S(2)}) %collective-permute-start.3) | collective-permute-done | bytes 32800 | tf_op jit(solution)/shard_map/ppermute | solution.py:18
  36.1 4.6 %select_maximum_fusion.4 = f32[40,136,136]{2,1,0:T(8,128)S(1)} fusion(f32[4,128,128]{2,1,0:T(8,128)} %copy-done.8, f32[32,128,128]{2,1,0:T(8,128)S(1)} %copy-done, f32[4,128,128]{2,1,0:T(8,128)} %collective-permute-done.5), kind=kLoop, calls=%fused_computation.8 | loop fusion | flops 11097600 | bytes 5580800 | tf_op jit(solution)/shard_map/concatenate | solution.py:16
  40.7 9.8 %fusion.23 = (f32[32,128,128]{2,1,0:T(8,128)}, f32[32,128,128]{2,1,0:T(8,128)}) fusion(f32[40,136,136]{2,1,0:T(8,128)S(1)} %select_maximum_fusion.4), kind=kLoop, calls=%fused_computation.66 | loop fusion | flops 11534336 | bytes 37748736 | tf_op jit(solution)/shard_map/add | solution.py:46
  51.5 2.1 constant_dynamic-update-slice_fusion.3
  53.7 2.0 fusion.30
  57.1 1.6 multiply_add_fusion.2
  58.8 1.5 stack.4
  60.3 10.7 %all-to-all-start = ((f32[16,32,8,128]{3,2,1,0:T(8,128)}), f32[16,32,8,128]{3,2,1,0:T(8,128)}, u32[]{:S(2)}, u32[]{:S(2)}) async-start(f32[16,32,8,128]{3,2,1,0:T(8,128)} %stack.4), calls=%async_computation | async-start | bytes 4194304 | tf_op jit(solution)/shard_map/all_to_all | solution.py:90
  72.0 1.9 collective-permute-start.10
  74.0 2.4 collective-permute-start.11
  76.4 2.1 collective-permute-start.7
  78.5 4.7 %collective-permute-start.6 = (f32[32,4,128]{2,1,0:T(4,128)S(1)}, f32[32,4,128]{2,1,0:T(4,128)S(1)}, u32[]{:S(2)}, u32[]{:S(2)}) collective-permute-start(f32[32,4,128]{2,1,0:T(4,128)S(1)} %get-tuple-element.26), channel_id=1, source_target_pairs={{0,16},{16,32},{32,48},{48,64},{64,80},{80,96},{96,112},{112,128},... | collective-permute-start | bytes 196616 | tf_op jit(solution)/shard_map/ppermute | solution.py:18
  83.2 31.6 %collective-permute-done.7 = f32[32,4,128]{2,1,0:T(4,128)S(1)} collective-permute-done((f32[32,4,128]{2,1,0:T(4,128)S(1)}, f32[32,4,128]{2,1,0:T(4,128)S(1)}, u32[]{:S(2)}, u32[]{:S(2)}) %collective-permute-start.7) | collective-permute-done | bytes 65568 | tf_op jit(solution)/shard_map/ppermute | solution.py:20
  114.8 3.7 %collective-permute-start.8 = (f32[4,16,128]{2,1,0:T(8,128)S(1)}, f32[4,16,128]{2,1,0:T(8,128)S(1)}, u32[]{:S(2)}, u32[]{:S(2)}) collective-permute-start(f32[4,16,128]{2,1,0:T(8,128)S(1)} %get-tuple-element.21), channel_id=1, source_target_pairs={{1,0},{2,1},{3,2},{4,3},{5,4},{6,5},{7,6},{8,7},{9,8},{10,9},{11,1... | collective-permute-start | bytes 98312 | tf_op jit(solution)/shard_map/ppermute | solution.py:20
  118.5 2.1 collective-permute-start.9
  120.6 6.5 %select_maximum_fusion.2 = f32[40,136,136]{2,1,0:T(8,128)} fusion(f32[4,128,128]{2,1,0:T(8,128)S(1)} %collective-permute-done.10, f32[32,128,128]{2,1,0:T(8,128)} %bitcast.32, f32[4,128,128]{2,1,0:T(8,128)S(1)} %collective-permute-done.11), kind=kLoop, calls=%fused_computation.6 | loop fusion | flops 11097600 | bytes 5580800 | tf_op jit(solution)/shard_map/concatenate | solution.py:16
  127.8 2.4 multiply_add_fusion
  130.2 1.6 stack.5
  131.7 5.6 %all-to-all-start.1 = ((f32[16,32,8,128]{3,2,1,0:T(8,128)}), f32[16,32,8,128]{3,2,1,0:T(8,128)}, u32[]{:S(2)}, u32[]{:S(2)}) async-start(f32[16,32,8,128]{3,2,1,0:T(8,128)} %stack.5), calls=%async_computation.1 | async-start | bytes 4194304 | tf_op jit(solution)/shard_map/all_to_all | solution.py:90
  137.3 47.9 %fusion.38 = f32[32,128,128]{2,1,0:T(8,128)} fusion(f32[1,32,128,128]{3,2,1,0:T(8,128)} %param.11, f32[1,32,128,128]{3,2,1,0:T(8,128)} %param.12, f32[16,32,8,128]{3,2,1,0:T(8,128)} %all-to-all-done, f32[32,128,128]{2,1,0:T(8,128)} %param.10, f32[32,128,128]{2,1,0:T(8,128)} %get-tuple-element.9, f32[32,128,128]{2,1,0:T(8,128)} %get-tuple-element.8, ...), kind=kLoop, calls=%fused_computation.90 | loop fusion | flops 47710208 | bytes 55050240 | tf_op jit(solution)/shard_map/add | solution.py:97
  186.3 6.6 %collective-permute-start.12 = (f32[4,128,128]{2,1,0:T(8,128)S(1)}, f32[4,128,128]{2,1,0:T(8,128)S(1)}, u32[]{:S(2)}, u32[]{:S(2)}) collective-permute-start(f32[4,128,128]{2,1,0:T(8,128)S(1)} %get-tuple-element.11), channel_id=1, source_target_pairs={{1,0},{2,1},{3,2},{4,3},{5,4},{6,5},{7,6},{8,7},{9,8},{10,9},{11,1... | collective-permute-start | bytes 786440 | tf_op jit(solution)/shard_map/ppermute | solution.py:20
  192.9 2.1 collective-permute-start.13
  195.0 1.7 collective-permute-done.12
  196.7 7.4 %collective-permute-done.13 = f32[4,128,128]{2,1,0:T(8,128)S(1)} collective-permute-done((f32[4,128,128]{2,1,0:T(8,128)S(1)}, f32[4,128,128]{2,1,0:T(8,128)S(1)}, u32[]{:S(2)}, u32[]{:S(2)}) %collective-permute-start.13) | collective-permute-done | bytes 262176 | tf_op jit(solution)/shard_map/ppermute | solution.py:18
  204.2 6.5 %select_maximum_fusion = f32[40,136,136]{2,1,0:T(8,128)} fusion(f32[4,128,128]{2,1,0:T(8,128)S(1)} %collective-permute-done.12, f32[32,128,128]{2,1,0:T(8,128)} %fusion.38, f32[4,128,128]{2,1,0:T(8,128)S(1)} %collective-permute-done.13), kind=kLoop, calls=%fused_computation.4 | loop fusion | flops 11097600 | bytes 5580800 | tf_op jit(solution)/shard_map/concatenate | solution.py:16
  210.7 48.8 %fusion.37 = f32[1,32,128,128]{3,2,1,0:T(8,128)} fusion(f32[1,32,128,128]{3,2,1,0:T(8,128)} %param.11, f32[16,32,8,128]{3,2,1,0:T(8,128)} %all-to-all-done.1, f32[32,128,128]{2,1,0:T(8,128)} %param.10, f32[32,128,128]{2,1,0:T(8,128)} %get-tuple-element.9, f32[32,128,128]{2,1,0:T(8,128)} %get-tuple-element.8, f32[32,128,128]{2,1,0:T(8,128)} %copy-done.2, ...), kind=kLoop, calls=%fused_computation.88 | loop fusion | flops 47710208 | bytes 55050240 | tf_op jit(solution)/shard_map/broadcast_in_dim | solution.py:102
  (49 shorter events, 12.5 us)
Async XLA Ops:
  0.6 33.6 %copy-start.3 = (f32[32,8,128]{2,1,0:T(8,128)S(1)}, f32[32,8,128]{2,1,0:T(8,128)}, u32[]{:S(2)}) copy-start(f32[32,8,128]{2,1,0:T(8,128)} %param.8) | copy-start | bytes 393220
  1.8 33.7 %collective-permute-start.4 = (f32[4,128,128]{2,1,0:T(8,128)S(1)}, f32[4,128,128]{2,1,0:T(8,128)S(1)}, u32[]{:S(2)}, u32[]{:S(2)}) collective-permute-start(f32[4,128,128]{2,1,0:T(8,128)S(1)} %get-tuple-element.17), channel_id=1, source_target_pairs={{1,0},{2,1},{3,2},{4,3},{5,4},{6,5},{7,6},{8,7},{9,8},{10,9},{11,1... | collective-permute-start | bytes 786440 | tf_op jit(solution)/shard_map/ppermute | solution.py:20
  7.0 29.2 %collective-permute-start.5 = (f32[4,128,128]{2,1,0:T(8,128)S(1)}, f32[4,128,128]{2,1,0:T(8,128)}, u32[]{:S(2)}, u32[]{:S(2)}) collective-permute-start(f32[4,128,128]{2,1,0:T(8,128)S(1)} %get-tuple-element.16), channel_id=1, source_target_pairs={{0,1},{1,2},{2,3},{3,4},{4,5},{5,6},{6,7},{7,8},{8,9},{9,10},{10,1... | collective-permute-start | bytes 786440 | tf_op jit(solution)/shard_map/ppermute | solution.py:18
  9.9 7.8 %collective-permute-start.1 = (f32[32,4,128]{2,1,0:T(4,128)S(1)}, f32[32,4,128]{2,1,0:T(4,128)S(1)}, u32[]{:S(2)}, u32[]{:S(2)}) collective-permute-start(f32[32,4,128]{2,1,0:T(4,128)S(1)} %get-tuple-element.29), channel_id=1, source_target_pairs={{16,0},{32,16},{48,32},{64,48},{80,64},{96,80},{112,96},{128,112},... | collective-permute-start | bytes 196616 | tf_op jit(solution)/shard_map/ppermute | solution.py:20
  11.8 6.7 %collective-permute-start = (f32[32,4,128]{2,1,0:T(4,128)S(1)}, f32[32,4,128]{2,1,0:T(4,128)S(1)}, u32[]{:S(2)}, u32[]{:S(2)}) collective-permute-start(f32[32,4,128]{2,1,0:T(4,128)S(1)} %get-tuple-element.28), channel_id=1, source_target_pairs={{0,16},{16,32},{32,48},{48,64},{64,80},{80,96},{96,112},{112,128},... | collective-permute-start | bytes 196616 | tf_op jit(solution)/shard_map/ppermute | solution.py:18
  16.7 19.5 %copy-start = (f32[32,128,128]{2,1,0:T(8,128)S(1)}, f32[32,128,128]{2,1,0:T(8,128)}, u32[]{:S(2)}) copy-start(f32[32,128,128]{2,1,0:T(8,128)} %param.9) | copy-start | bytes 6291460
  19.3 8.1 %collective-permute-start.2 = (f32[4,16,128]{2,1,0:T(8,128)S(1)}, f32[4,16,128]{2,1,0:T(8,128)S(1)}, u32[]{:S(2)}, u32[]{:S(2)}) collective-permute-start(f32[4,16,128]{2,1,0:T(8,128)S(1)} %get-tuple-element.25), channel_id=1, source_target_pairs={{1,0},{2,1},{3,2},{4,3},{5,4},{6,5},{7,6},{8,7},{9,8},{10,9},{11,1... | collective-permute-start | bytes 98312 | tf_op jit(solution)/shard_map/ppermute | solution.py:20
  25.4 8.8 %collective-permute-start.3 = (f32[4,16,128]{2,1,0:T(8,128)S(1)}, f32[4,16,128]{2,1,0:T(8,128)S(1)}, u32[]{:S(2)}, u32[]{:S(2)}) collective-permute-start(f32[4,16,128]{2,1,0:T(8,128)S(1)} %get-tuple-element.24), channel_id=1, source_target_pairs={{0,1},{1,2},{2,3},{3,4},{4,5},{5,6},{6,7},{7,8},{8,9},{9,10},{10,1... | collective-permute-start | bytes 98312 | tf_op jit(solution)/shard_map/ppermute | solution.py:18
  27.4 0.7 copy-start.6
  35.4 0.7 copy-start.8
  51.5 2.2 copy-start.9
  53.7 3.4 %copy-start.1 = (f32[32,128,128]{2,1,0:T(8,128)S(1)}, f32[32,128,128]{2,1,0:T(8,128)}, u32[]{:S(2)}) copy-start(f32[32,128,128]{2,1,0:T(8,128)} %param.9) | copy-start | bytes 6291460
  53.7 3.4 %copy-start.5 = (f32[36,16,128]{2,1,0:T(8,128)S(1)}, f32[36,16,128]{2,1,0:T(8,128)}, u32[]{:S(2)}) copy-start(f32[36,16,128]{2,1,0:T(8,128)} %get-tuple-element.23) | copy-start | bytes 884740
  53.7 3.4 %copy-start.7 = (f32[32,12,128]{2,1,0:T(8,128)S(1)}, f32[32,12,128]{2,1,0:T(8,128)}, u32[]{:S(2)}) copy-start(f32[32,12,128]{2,1,0:T(8,128)} %copy-done.6) | copy-start | bytes 589828
  53.7 3.4 %copy-start.10 = (f32[32,8,128]{2,1,0:T(8,128)S(1)}, f32[32,8,128]{2,1,0:T(8,128)}, u32[]{:S(2)}) copy-start(f32[32,8,128]{2,1,0:T(8,128)} %param.7) | copy-start | bytes 393220
  55.7 1.4 copy-start.2
  58.7 69.0 %copy-start.4 = (f32[32,8,128]{2,1,0:T(8,128)}, f32[32,8,128]{2,1,0:T(8,128)S(1)}, u32[]{:S(2)}) copy-start(f32[32,8,128]{2,1,0:T(8,128)S(1)} %get-tuple-element.6) | copy-start | bytes 393220
  60.3 69.9 %all-to-all-start = ((f32[16,32,8,128]{3,2,1,0:T(8,128)}), f32[16,32,8,128]{3,2,1,0:T(8,128)}, u32[]{:S(2)}, u32[]{:S(2)}) async-start(f32[16,32,8,128]{3,2,1,0:T(8,128)} %stack.4), calls=%async_computation | async-start | bytes 4194304 | tf_op jit(solution)/shard_map/all_to_all | solution.py:90
  72.0 48.6 %collective-permute-start.10 = (f32[4,128,128]{2,1,0:T(8,128)S(1)}, f32[4,128,128]{2,1,0:T(8,128)S(1)}, u32[]{:S(2)}, u32[]{:S(2)}) collective-permute-start(f32[4,128,128]{2,1,0:T(8,128)S(1)} %get-tuple-element.13), channel_id=1, source_target_pairs={{1,0},{2,1},{3,2},{4,3},{5,4},{6,5},{7,6},{8,7},{9,8},{10,9},{11,1... | collective-permute-start | bytes 786440 | tf_op jit(solution)/shard_map/ppermute | solution.py:20
  74.0 46.7 %collective-permute-start.11 = (f32[4,128,128]{2,1,0:T(8,128)S(1)}, f32[4,128,128]{2,1,0:T(8,128)S(1)}, u32[]{:S(2)}, u32[]{:S(2)}) collective-permute-start(f32[4,128,128]{2,1,0:T(8,128)S(1)} %get-tuple-element.12), channel_id=1, source_target_pairs={{0,1},{1,2},{2,3},{3,4},{4,5},{5,6},{6,7},{7,8},{8,9},{9,10},{10,1... | collective-permute-start | bytes 786440 | tf_op jit(solution)/shard_map/ppermute | solution.py:18
  76.4 38.4 %collective-permute-start.7 = (f32[32,4,128]{2,1,0:T(4,128)S(1)}, f32[32,4,128]{2,1,0:T(4,128)S(1)}, u32[]{:S(2)}, u32[]{:S(2)}) collective-permute-start(f32[32,4,128]{2,1,0:T(4,128)S(1)} %get-tuple-element.27), channel_id=1, source_target_pairs={{16,0},{32,16},{48,32},{64,48},{80,64},{96,80},{112,96},{128,112},... | collective-permute-start | bytes 196616 | tf_op jit(solution)/shard_map/ppermute | solution.py:20
  78.5 36.3 %collective-permute-start.6 = (f32[32,4,128]{2,1,0:T(4,128)S(1)}, f32[32,4,128]{2,1,0:T(4,128)S(1)}, u32[]{:S(2)}, u32[]{:S(2)}) collective-permute-start(f32[32,4,128]{2,1,0:T(4,128)S(1)} %get-tuple-element.26), channel_id=1, source_target_pairs={{0,16},{16,32},{32,48},{48,64},{64,80},{80,96},{96,112},{112,128},... | collective-permute-start | bytes 196616 | tf_op jit(solution)/shard_map/ppermute | solution.py:18
  114.8 12.3 %collective-permute-start.8 = (f32[4,16,128]{2,1,0:T(8,128)S(1)}, f32[4,16,128]{2,1,0:T(8,128)S(1)}, u32[]{:S(2)}, u32[]{:S(2)}) collective-permute-start(f32[4,16,128]{2,1,0:T(8,128)S(1)} %get-tuple-element.21), channel_id=1, source_target_pairs={{1,0},{2,1},{3,2},{4,3},{5,4},{6,5},{7,6},{8,7},{9,8},{10,9},{11,1... | collective-permute-start | bytes 98312 | tf_op jit(solution)/shard_map/ppermute | solution.py:20
  118.5 8.8 %collective-permute-start.9 = (f32[4,16,128]{2,1,0:T(8,128)S(1)}, f32[4,16,128]{2,1,0:T(8,128)S(1)}, u32[]{:S(2)}, u32[]{:S(2)}) collective-permute-start(f32[4,16,128]{2,1,0:T(8,128)S(1)} %get-tuple-element.20), channel_id=1, source_target_pairs={{0,1},{1,2},{2,3},{3,4},{4,5},{5,6},{6,7},{7,8},{8,9},{9,10},{10,1... | collective-permute-start | bytes 98312 | tf_op jit(solution)/shard_map/ppermute | solution.py:18
  131.7 78.9 %all-to-all-start.1 = ((f32[16,32,8,128]{3,2,1,0:T(8,128)}), f32[16,32,8,128]{3,2,1,0:T(8,128)}, u32[]{:S(2)}, u32[]{:S(2)}) async-start(f32[16,32,8,128]{3,2,1,0:T(8,128)} %stack.5), calls=%async_computation.1 | async-start | bytes 4194304 | tf_op jit(solution)/shard_map/all_to_all | solution.py:90
  186.3 10.4 %collective-permute-start.12 = (f32[4,128,128]{2,1,0:T(8,128)S(1)}, f32[4,128,128]{2,1,0:T(8,128)S(1)}, u32[]{:S(2)}, u32[]{:S(2)}) collective-permute-start(f32[4,128,128]{2,1,0:T(8,128)S(1)} %get-tuple-element.11), channel_id=1, source_target_pairs={{1,0},{2,1},{3,2},{4,3},{5,4},{6,5},{7,6},{8,7},{9,8},{10,9},{11,1... | collective-permute-start | bytes 786440 | tf_op jit(solution)/shard_map/ppermute | solution.py:20
  192.9 11.3 %collective-permute-start.13 = (f32[4,128,128]{2,1,0:T(8,128)S(1)}, f32[4,128,128]{2,1,0:T(8,128)S(1)}, u32[]{:S(2)}, u32[]{:S(2)}) collective-permute-start(f32[4,128,128]{2,1,0:T(8,128)S(1)} %get-tuple-element.10), channel_id=1, source_target_pairs={{0,1},{1,2},{2,3},{3,4},{4,5},{5,6},{6,7},{7,8},{8,9},{9,10},{10,1... | collective-permute-start | bytes 786440 | tf_op jit(solution)/shard_map/ppermute | solution.py:18
